TPU v7x, 256 devices: a whole 4x4x8 slice. The times are simulated.
256 devices in a mesh: slab: 32 (over z, x), coil: 8 (over y, core).
Axes of the slice: x: 4, y: 4, z: 8, core: 2. Of those that a mesh axis runs over, the one named last changes fastest.
Arguments:
- noisy: float32 [2, 64, 256, 128], P(None, 'slab', 'coil'), may hold values from -6 to 6
- step_index: int32 [], replicated, may hold values from 200 to 599
- w_in: bfloat16 [3, 3, 3, 32, 2], replicated, may hold values from -0.875 to 0.875
- w_mid: bfloat16 [3, 3, 3, 32, 32], replicated, may hold values from -0.21875 to 0.21875
- w_out: bfloat16 [3, 3, 3, 2, 32], replicated, may hold values from -0.21875 to 0.21875
- time_weight: float32 [32, 32], replicated, may hold values from -1 to 1
- sens: float32 [16, 2, 64, 256, 128], P('coil', None, 'slab')
- kdata: float32 [16, 2, 64, 256, 128], P('coil', None, None, 'slab'), may hold values from -4 to 4
- mask: int32 [64, 256], P(None, 'slab'), may hold values from 0 to 1, as said below
Outputs:
- recon: float32 [2, 64, 256, 128], P(None, 'slab', 'coil')
- next_sample: float32 [2, 64, 256, 128], P(None, 'slab', 'coil')
Inputs may be any that keep to these rules, and one draw needn't show every extreme that they name: mask[kz, ky] is 1 wherever min(kz, 64 - kz) < max(1, 4) and min(ky, 256 - ky) < max(1, 8); every other entry is 1 with chance one in three.
All inputs are finite; a program needn't handle non-finite values.
Results may differ from a plain program's by a relative error of at most 0.0023.
Values may be sent and summed in bfloat16 or wider, within the bound.
No kernel may reach another device: no remote copies, remote signals or barrier semaphores. Data moves between devices by JAX's collectives and lax.ppermute only.
A program may use at most 64 MiB of HBM per device.

v0:
```python
import math
import jax
import jax.numpy as jnp
from jax import lax
from jax.sharding import PartitionSpec as P

ITERS = 2
STEPS = 1000
STRIDE = 20
REG_WEIGHT = 0.5
HIGHEST_PRECISION = lax.Precision.HIGHEST


def extended(cells, sides, width):
    for axis, dim in sides:
        count = lax.axis_size(axis)
        ends = count - 1
        head = lax.slice_in_dim(cells, 0, width, axis=dim)
        tail = lax.slice_in_dim(cells, cells.shape[dim] - width, cells.shape[dim], axis=dim)
        cells = jnp.concatenate(
            [
                lax.ppermute(tail, axis, [(i, (i + 1) % count) for i in range(ends)]),
                cells,
                lax.ppermute(head, axis, [((i + 1) % count, i) for i in range(ends)]),
            ],
            axis=dim,
        )
    return cells


def plan_level(step_value):
    angle = (step_value / STEPS + 0.008) / 1.008 * (math.pi / 2)
    return jnp.cos(angle) ** 2


def time_bias(step_value, time_weight):
    half = time_weight.shape[0] // 2
    freqs = jnp.exp(-math.log(10000.0) * jnp.arange(half, dtype=jnp.float32) / half)
    phase = step_value * freqs
    embed = jnp.concatenate([jnp.sin(phase), jnp.cos(phase)])
    return jnp.dot(embed, time_weight, precision=HIGHEST_PRECISION)


def conv_layer(inputs, weights):
    padded = extended(inputs, (("slab", 1), ("coil", 2)), 1)
    kernel = jnp.transpose(weights, (3, 4, 0, 1, 2))
    result = lax.conv_general_dilated(
        padded[None],
        kernel,
        (1, 1, 1),
        ((0, 0), (0, 0), (1, 1)),
        dimension_numbers=("NCDHW", "OIDHW", "NCDHW"),
        preferred_element_type=jnp.float32,
    )
    return result[0]


def dft_blocks(length, inverse):
    index = jnp.arange(length, dtype=jnp.int32)
    product = index[:, None] * index[None, :] % length
    theta = product.astype(jnp.float32) * (2.0 * math.pi / length)
    cosine = jnp.cos(theta) / math.sqrt(length)
    sine = jnp.sin(theta) / math.sqrt(length)
    if inverse:
        sine = -sine
    upper = jnp.stack([cosine, sine], axis=1)
    lower = jnp.stack([-sine, cosine], axis=1)
    return jnp.stack([upper, lower], axis=0)


def along_last(data, blocks):
    return jnp.einsum("pkqn,cqzyn->cpzyk", blocks, data, precision=HIGHEST_PRECISION)


def along_rows(data, blocks):
    return jnp.einsum("pkqn,cqzny->cpzky", blocks, data, precision=HIGHEST_PRECISION)


def along_depth(data, blocks):
    return jnp.einsum("pkqn,cqnyx->cpkyx", blocks, data, precision=HIGHEST_PRECISION)


def times_sens(sens, image):
    real_part = sens[:, 0] * image[0] - sens[:, 1] * image[1]
    imag_part = sens[:, 0] * image[1] + sens[:, 1] * image[0]
    return jnp.stack([real_part, imag_part], axis=1)


def times_conj(sens, images):
    real_part = jnp.sum(sens[:, 0] * images[:, 0] + sens[:, 1] * images[:, 1], axis=0)
    imag_part = jnp.sum(sens[:, 0] * images[:, 1] - sens[:, 1] * images[:, 0], axis=0)
    return jnp.stack([real_part, imag_part])


def coil_term(image_full, sens, kdata_x, weight, blocks, with_data):
    forward_y, forward_z, inverse_y, inverse_z = blocks
    coil_images = times_sens(sens, image_full)
    spectrum = along_rows(coil_images, forward_y)
    pencils = lax.all_to_all(
        spectrum.astype(jnp.bfloat16), "slab", split_axis=3, concat_axis=2, tiled=True
    ).astype(jnp.float32)
    kspace = along_depth(pencils, forward_z)
    if with_data:
        kspace = weight * (kdata_x - kspace)
    else:
        kspace = weight * kspace
    back = along_depth(kspace, inverse_z)
    slabs = lax.all_to_all(
        back.astype(jnp.bfloat16), "slab", split_axis=2, concat_axis=3, tiled=True
    ).astype(jnp.float32)
    images = along_rows(slabs, inverse_y)
    return times_conj(sens, images)


def combine_coils(partial_value):
    count = lax.axis_size("coil")
    pieces = lax.all_to_all(partial_value, "coil", split_axis=2, concat_axis=0, tiled=True)
    pieces = pieces.reshape((count, partial_value.shape[0]) + pieces.shape[1:])
    return jnp.sum(pieces, axis=0)


def gather_rows(value):
    return lax.all_gather(value, "coil", axis=2, tiled=True)


def global_sums(values):
    axes = ("slab", "coil")
    count = lax.axis_size("slab") * lax.axis_size("coil")
    spread = jnp.broadcast_to(values[None], (count,) + values.shape)
    return jnp.sum(lax.all_to_all(spread, axes, split_axis=0, concat_axis=0, tiled=True), axis=0)


def body(noisy, step_index, w_in, w_mid, w_out, time_weight, sens, kdata, mask):
    step_value = step_index.astype(jnp.float32)
    signal_level = plan_level(step_value)
    prior_level = plan_level(step_value - STRIDE)
    bias = time_bias(step_value, time_weight)
    hidden = jax.nn.silu(
        conv_layer(noisy.astype(jnp.bfloat16), w_in) + bias[:, None, None, None]
    ).astype(jnp.bfloat16)
    mixed = (hidden.astype(jnp.float32) + jax.nn.silu(conv_layer(hidden, w_mid))).astype(
        jnp.bfloat16
    )
    noise_pred = conv_layer(mixed, w_out)
    estimate = (noisy - jnp.sqrt(1.0 - signal_level) * noise_pred) / jnp.sqrt(signal_level)
    depth_full = kdata.shape[2]
    rows_full = sens.shape[3]
    width = sens.shape[4]
    blocks = (
        dft_blocks(rows_full, False),
        dft_blocks(depth_full, False),
        dft_blocks(rows_full, True),
        dft_blocks(depth_full, True),
    )
    kdata_x = along_last(kdata, dft_blocks(width, True))
    weight = mask.astype(jnp.float32)[None, None, :, :, None]

    def operator(image, with_data):
        return combine_coils(
            coil_term(gather_rows(image), sens, kdata_x, weight, blocks, with_data)
        )

    solution = estimate
    residual = operator(estimate, True)
    direction = residual
    norm_now = None
    for iteration in range(ITERS):
        final_turn = iteration + 1 == ITERS
        image = operator(direction, False) + REG_WEIGHT * direction
        if norm_now is None:
            sums = global_sums(
                jnp.stack([jnp.sum(residual * residual), jnp.sum(direction * image)])
            )
            norm_now, curvature = (sums[0], sums[1])
        else:
            curvature = global_sums(jnp.stack([jnp.sum(direction * image)]))[0]
        step_size = norm_now / curvature
        solution = solution + step_size * direction
        if not final_turn:
            residual = residual - step_size * image
            norm_next = global_sums(jnp.stack([jnp.sum(residual * residual)]))[0]
            direction = residual + norm_next / norm_now * direction
            norm_now = norm_next
    recon = solution
    next_sample = jnp.sqrt(prior_level) * recon + jnp.sqrt(1.0 - prior_level) * noise_pred
    return (recon, next_sample)


def solution(mesh):
    return jax.shard_map(
        body,
        mesh=mesh,
        in_specs=(
            P(None, "slab", "coil", None),
            P(),
            P(),
            P(),
            P(),
            P(),
            P("coil", None, "slab", None, None),
            P("coil", None, None, "slab", None),
            P(None, "slab"),
        ),
        out_specs=(P(None, "slab", "coil", None), P(None, "slab", "coil", None)),
        check_vma=False,
    )
```

profile of v0, /device:TPU:1, one launch (start us, length us, event | category | flops | bytes accessed | tf_op | source)
XLA Modules:
  0.0 684.9 jit_solution(6342718819612224770)
XLA Ops:
  22.7 7.8 %broadcast_select_fusion.1 = f32[2,32,8,17,32]{4,2,3,1,0:T(8,128)S(1)} fusion(pred[8,17]{0,1:T(8,128)(4,1)} %constant.113, bf16[3,3,3,32,2]{3,4,2,1,0:T(2,128)(2,1)} %param.11, bf16[2,4,34,1,7,2]{4,0,5,2,1,3:T(2,128)(2,1)S(1)} %slice.155, bf16[2,4,34,1,8,17]{4,0,5,2,1,3:T(2,128)(2,1)S(1)} %copy.378), kind=kOutput, calls=%fused_computation.23 | convolution fusion | flops 30607616 | bytes 1199304 | tf_op jit(solution)/shard_map/conv_general_dilated | solution.py:47
  75.3 8.1 %copy.497 = bf16[32,4,34,1,128]{2,0,4,1,3:T(8,128)(2,1)} copy(bf16[32,4,34,1,128]{0,2,4,1,3:T(8,128)(2,1)} %maximum_bitcast_fusion) | data formatting | bytes 2228224
  88.5 8.7 %copy.386 = bf16[32,4,34,1,8,17]{0,4,5,2,1,3:T(8,128)(2,1)} copy(bf16[32,4,34,1,8,17]{2,0,5,4,1,3:T(8,128)(2,1)} %bitcast.328) | data formatting | bytes 2367488 | tf_op jit(solution)/shard_map/conv_general_dilated | solution.py:47
  98.5 8.6 %broadcast_select_fusion = f32[2,32,8,17,32]{4,2,3,1,0:T(8,128)S(1)} fusion(pred[8,17]{0,1:T(8,128)(4,1)S(1)} %copy-done.25, bf16[3,3,3,32,32]{4,3,2,1,0:T(8,128)(2,1)S(1)} %copy-done.26, bf16[32,4,34,1,7,2]{0,4,5,2,1,3:T(8,128)(2,1)S(1)} %slice.159, bf16[32,4,34,1,8,17]{0,4,5,2,1,3:T(8,128)(2,1)} %copy.386), kind=kOutput, calls=%fused_computation.22 | convolution fusion | flops 485543936 | bytes 2475144 | tf_op jit(solution)/shard_map/conv_general_dilated | solution.py:47
  156.4 8.1 %copy.498 = bf16[32,4,34,1,128]{2,0,4,1,3:T(8,128)(2,1)} copy(bf16[32,4,34,1,128]{0,2,4,1,3:T(8,128)(2,1)} %maximum_bitcast_fusion.1) | data formatting | bytes 2228224
  169.6 8.7 %copy.394 = bf16[32,4,34,1,8,17]{0,4,5,2,1,3:T(8,128)(2,1)} copy(bf16[32,4,34,1,8,17]{2,0,5,4,1,3:T(8,128)(2,1)} %bitcast.327) | data formatting | bytes 2367488 | tf_op jit(solution)/shard_map/conv_general_dilated | solution.py:47
  179.5 139.8 %fusion.11 = f32[2,32,8,17,2]{2,4,3,1,0:T(2,128)} fusion(bf16[3,3,3,2,32]{4,3,2,1,0:T(2,128)(2,1)S(1)} %copy-done.27, bf16[32,4,34,1,7,2]{0,4,5,2,1,3:T(8,128)(2,1)S(1)} %slice.163, bf16[32,4,34,1,8,17]{0,4,5,2,1,3:T(8,128)(2,1)} %copy.394), kind=kOutput, calls=%fused_computation.11 | convolution fusion | flops 34050048 | bytes 1378688 | tf_op jit(solution)/shard_map/conv_general_dilated | solution.py:47
  325.5 14.1 %all_gather.9 = f32[2,2,256,128]{3,1,0,2:T(2,128)S(1)} all-gather(f32[2,2,32,128]{3,1,0,2:T(2,128)S(1)} %fusion.74), channel_id=1, replica_groups=mesh['slab'=32,'coil'=8] {'coil'}, dimensions={2}, use_global_device_ids=true | all-gather | bytes 589824 | tf_op jit(solution)/shard_map/all_gather | solution.py:123
  350.0 14.7 %all-to-all-start = ((bf16[2,2,2,256,128]{4,1,2,0,3:T(2,128)(2,1)}), bf16[2,2,2,256,128]{4,1,2,0,3:T(2,128)(2,1)S(1)}, u32[]{:S(2)}, u32[]{:S(2)}) async-start(bf16[2,2,2,256,128]{4,1,2,0,3:T(2,128)(2,1)} %copy.404), calls=%async_computation | async-start | bytes 1048576 | tf_op jit(solution)/shard_map/all_to_all | solution.py:99
  369.0 12.5 %all-to-all-done = bf16[2,2,2,256,128]{4,1,2,0,3:T(2,128)(2,1)S(1)} async-done(((bf16[2,2,2,256,128]{4,1,2,0,3:T(2,128)(2,1)}), bf16[2,2,2,256,128]{4,1,2,0,3:T(2,128)(2,1)S(1)}, u32[]{:S(2)}, u32[]{:S(2)}) %all-to-all-start) | async-done | bytes 524320 | tf_op jit(solution)/shard_map/all_to_all | solution.py:99
  385.3 20.3 %all_to_all.162 = bf16[2,2,64,8,128]{4,1,3,0,2:T(2,128)(2,1)S(1)} all-to-all(bf16[2,2,64,8,128]{4,1,3,0,2:T(2,128)(2,1)S(1)} %copy.408), channel_id=1, replica_groups=mesh['slab'=32,'coil'=8] {'slab'}, dimensions={2} | all-to-all | bytes 1048576 | tf_op jit(solution)/shard_map/all_to_all | solution.py:108
  410.0 16.8 %all_to_all.163 = f32[2,2,256,128]{3,1,0,2:T(2,128)} all-to-all(f32[2,2,256,128]{3,1,0,2:T(2,128)} %copy.412), channel_id=1, replica_groups=mesh['slab'=32,'coil'=8] {'coil'}, dimensions={2} | all-to-all | bytes 1048576 | tf_op jit(solution)/shard_map/all_to_all | solution.py:117
  428.1 14.2 %all_gather.10 = f32[2,2,256,128]{3,1,0,2:T(2,128)S(1)} all-gather(f32[2,2,32,128]{3,1,0,2:T(2,128)S(1)} %reduce_sum.146), channel_id=1, replica_groups=mesh['slab'=32,'coil'=8] {'coil'}, dimensions={2}, use_global_device_ids=true | all-gather | bytes 589824 | tf_op jit(solution)/shard_map/all_gather | solution.py:123
  453.8 21.1 %all_to_all.164 = bf16[2,2,2,256,128]{4,1,2,0,3:T(2,128)(2,1)S(1)} all-to-all(bf16[2,2,2,256,128]{4,1,2,0,3:T(2,128)(2,1)} %copy.415), channel_id=1, replica_groups=mesh['slab'=32,'coil'=8] {'slab'}, dimensions={3} | all-to-all | bytes 1048576 | tf_op jit(solution)/shard_map/all_to_all | solution.py:99
  478.3 20.3 %all_to_all.165 = bf16[2,2,64,8,128]{4,1,3,0,2:T(2,128)(2,1)S(1)} all-to-all(bf16[2,2,64,8,128]{4,1,3,0,2:T(2,128)(2,1)S(1)} %copy.419), channel_id=1, replica_groups=mesh['slab'=32,'coil'=8] {'slab'}, dimensions={2} | all-to-all | bytes 1048576 | tf_op jit(solution)/shard_map/all_to_all | solution.py:108
  503.0 16.8 %all_to_all.166 = f32[2,2,256,128]{3,1,0,2:T(2,128)} all-to-all(f32[2,2,256,128]{3,1,0,2:T(2,128)} %copy.423), channel_id=1, replica_groups=mesh['slab'=32,'coil'=8] {'coil'}, dimensions={2} | all-to-all | bytes 1048576 | tf_op jit(solution)/shard_map/all_to_all | solution.py:117
  523.3 19.5 %all_to_all.167 = f32[256,1,2]{2,1,0:T(1,128)} all-to-all(f32[256,1,2]{2,1,0:T(1,128)S(1)} %broadcast_in_dim.15), channel_id=1, replica_groups=mesh['slab'=32,'coil'=8] {'slab','coil'}, dimensions={0} | all-to-all | bytes 4096 | tf_op jit(solution)/shard_map/all_to_all | solution.py:130
  548.7 19.5 %all_to_all.168 = f32[256,1,1]{2,1,0:T(1,128)} all-to-all(f32[256,1,1]{2,1,0:T(1,128)S(1)} %broadcast_in_dim.16), channel_id=1, replica_groups=mesh['slab'=32,'coil'=8] {'slab','coil'}, dimensions={0} | all-to-all | bytes 2048 | tf_op jit(solution)/shard_map/all_to_all | solution.py:130
  572.2 13.6 %all_gather.11 = f32[2,2,256,128]{3,1,0,2:T(2,128)S(1)} all-gather(f32[2,2,32,128]{3,1,0,2:T(2,128)S(1)} %multiply_add_fusion.4), channel_id=1, replica_groups=mesh['slab'=32,'coil'=8] {'coil'}, dimensions={2}, use_global_device_ids=true | all-gather | bytes 589824 | tf_op jit(solution)/shard_map/all_gather | solution.py:123
  597.4 21.0 %all_to_all.169 = bf16[2,2,2,256,128]{4,1,2,0,3:T(2,128)(2,1)S(1)} all-to-all(bf16[2,2,2,256,128]{4,1,2,0,3:T(2,128)(2,1)} %copy.428), channel_id=1, replica_groups=mesh['slab'=32,'coil'=8] {'slab'}, dimensions={3} | all-to-all | bytes 1048576 | tf_op jit(solution)/shard_map/all_to_all | solution.py:99
  621.8 20.3 %all_to_all.170 = bf16[2,2,64,8,128]{4,1,3,0,2:T(2,128)(2,1)S(1)} all-to-all(bf16[2,2,64,8,128]{4,1,3,0,2:T(2,128)(2,1)S(1)} %copy.432), channel_id=1, replica_groups=mesh['slab'=32,'coil'=8] {'slab'}, dimensions={2} | all-to-all | bytes 1048576 | tf_op jit(solution)/shard_map/all_to_all | solution.py:108
  644.0 15.2 %all_to_all.171 = f32[2,2,256,128]{3,1,0,2:T(2,128)S(1)} all-to-all(f32[2,2,256,128]{3,1,0,2:T(2,128)S(1)} %copy.436), channel_id=1, replica_groups=mesh['slab'=32,'coil'=8] {'coil'}, dimensions={2} | all-to-all | bytes 1048576 | tf_op jit(solution)/shard_map/all_to_all | solution.py:117
  661.4 6.5 all-to-all-start.11
  668.3 12.6 %all-to-all-done.11 = f32[256,1,1]{2,1,0:T(1,128)S(1)} async-done(((f32[256,1,1]{2,1,0:T(1,128)}), f32[256,1,1]{2,1,0:T(1,128)S(1)}, u32[]{:S(2)}, u32[]{:S(2)}) %all-to-all-start.11) | async-done | bytes 1056 | tf_op jit(solution)/shard_map/all_to_all | solution.py:130
  (206 shorter events, 209.2 us)
Async XLA Ops:
  0.6 366.3 %copy-start = (f32[2,2,64,8,128]{4,3,2,1,0:T(8,128)S(1)}, f32[2,2,64,8,128]{4,3,2,1,0:T(8,128)}, u32[]{:S(2)}) copy-start(f32[2,2,64,8,128]{4,3,2,1,0:T(8,128)} %param.16) | copy-start | bytes 3145732
  1.6 5.9 collective-permute-start
  5.5 4.5 collective-permute-start.1
  10.0 8.1 %collective-permute-start.2 = (bf16[2,4,1,128]{3,2,1,0:T(2,128)(2,1)S(1)}, bf16[2,4,1,128]{3,2,1,0:T(2,128)(2,1)S(1)}, u32[]{:S(2)}, u32[]{:S(2)}) collective-permute-start(bf16[2,4,1,128]{3,2,1,0:T(2,128)(2,1)S(1)} %get-tuple-element.62), channel_id=1, source_target_pairs={{0,1},{1,2},{2,3},{3,4},{4,5},{5,6},{6,7},{8,9},{9,10},{10,11},{11... | collective-permute-start | bytes 6152 | tf_op jit(solution)/shard_map/ppermute | solution.py:22
  15.2 4.9 collective-permute-start.3
  36.8 10.5 %collective-permute-start.4 = (bf16[32,1,32,128]{3,2,1,0:T(8,128)(2,1)S(1)}, bf16[32,1,32,128]{3,2,1,0:T(8,128)(2,1)}, u32[]{:S(2)}, u32[]{:S(2)}) collective-permute-start(bf16[32,1,32,128]{3,2,1,0:T(8,128)(2,1)S(1)} %copy.380), channel_id=1, source_target_pairs={{0,8},{8,16},{16,24},{24,32},{32,40},{40,48},{48,56},{56,64},{64,7... | collective-permute-start | bytes 786440 | tf_op jit(solution)/shard_map/ppermute | solution.py:22
  44.2 9.1 %collective-permute-start.5 = (bf16[32,1,32,128]{3,2,1,0:T(8,128)(2,1)}, bf16[32,1,32,128]{3,2,1,0:T(8,128)(2,1)}, u32[]{:S(2)}, u32[]{:S(2)}) collective-permute-start(bf16[32,1,32,128]{3,2,1,0:T(8,128)(2,1)} %copy.381), channel_id=1, source_target_pairs={{8,0},{16,8},{24,16},{32,24},{40,32},{48,40},{56,48},{64,56},{72,6... | collective-permute-start | bytes 786440 | tf_op jit(solution)/shard_map/ppermute | solution.py:24
  58.9 7.7 %collective-permute-start.6 = (bf16[32,4,1,128]{0,2,3,1:T(2,128)(2,1)S(1)}, bf16[32,4,1,128]{0,2,3,1:T(2,128)(2,1)S(1)}, u32[]{:S(2)}, u32[]{:S(2)}) collective-permute-start(bf16[32,4,1,128]{0,2,3,1:T(2,128)(2,1)S(1)} %get-tuple-element.28), channel_id=1, source_target_pairs={{0,1},{1,2},{2,3},{3,4},{4,5},{5,6},{6,7},{8,9},{9,10},{10,11},{11... | collective-permute-start | bytes 98312 | tf_op jit(solution)/shard_map/ppermute | solution.py:22
  63.0 7.7 %collective-permute-start.7 = (bf16[32,4,1,128]{0,2,3,1:T(2,128)(2,1)S(1)}, bf16[32,4,1,128]{0,2,3,1:T(2,128)(2,1)S(1)}, u32[]{:S(2)}, u32[]{:S(2)}) collective-permute-start(bf16[32,4,1,128]{0,2,3,1:T(2,128)(2,1)S(1)} %get-tuple-element.29), channel_id=1, source_target_pairs={{1,0},{2,1},{3,2},{4,3},{5,4},{6,5},{7,6},{9,8},{10,9},{11,10},{12... | collective-permute-start | bytes 98312 | tf_op jit(solution)/shard_map/ppermute | solution.py:24
  115.4 11.5 %collective-permute-start.8 = (bf16[32,1,32,128]{3,2,1,0:T(8,128)(2,1)}, bf16[32,1,32,128]{3,2,1,0:T(8,128)(2,1)}, u32[]{:S(2)}, u32[]{:S(2)}) collective-permute-start(bf16[32,1,32,128]{3,2,1,0:T(8,128)(2,1)} %copy.388), channel_id=1, source_target_pairs={{0,8},{8,16},{16,24},{24,32},{32,40},{40,48},{48,56},{56,64},{64,7... | collective-permute-start | bytes 786440 | tf_op jit(solution)/shard_map/ppermute | solution.py:22
  123.2 7.6 %collective-permute-start.9 = (bf16[32,1,32,128]{3,2,1,0:T(8,128)(2,1)}, bf16[32,1,32,128]{3,2,1,0:T(8,128)(2,1)}, u32[]{:S(2)}, u32[]{:S(2)}) collective-permute-start(bf16[32,1,32,128]{3,2,1,0:T(8,128)(2,1)} %copy.389), channel_id=1, source_target_pairs={{8,0},{16,8},{24,16},{32,24},{40,32},{48,40},{56,48},{64,56},{72,6... | collective-permute-start | bytes 786440 | tf_op jit(solution)/shard_map/ppermute | solution.py:24
  137.0 12.9 %collective-permute-start.10 = (bf16[32,4,1,128]{0,2,3,1:T(2,128)(2,1)}, bf16[32,4,1,128]{0,2,3,1:T(2,128)(2,1)}, u32[]{:S(2)}, u32[]{:S(2)}) collective-permute-start(bf16[32,4,1,128]{0,2,3,1:T(2,128)(2,1)} %get-tuple-element.26), channel_id=1, source_target_pairs={{0,1},{1,2},{2,3},{3,4},{4,5},{5,6},{6,7},{8,9},{9,10},{10,11},{11... | collective-permute-start | bytes 98312 | tf_op jit(solution)/shard_map/ppermute | solution.py:22
  142.1 8.0 %collective-permute-start.11 = (bf16[32,4,1,128]{0,2,3,1:T(2,128)(2,1)}, bf16[32,4,1,128]{0,2,3,1:T(2,128)(2,1)}, u32[]{:S(2)}, u32[]{:S(2)}) collective-permute-start(bf16[32,4,1,128]{0,2,3,1:T(2,128)(2,1)} %get-tuple-element.27), channel_id=1, source_target_pairs={{1,0},{2,1},{3,2},{4,3},{5,4},{6,5},{7,6},{9,8},{10,9},{11,10},{12... | collective-permute-start | bytes 98312 | tf_op jit(solution)/shard_map/ppermute | solution.py:24
  319.3 24.9 %copy-start.2 = (f32[2,1,2,256,128]{3,4,1,2,0:T(8,128)S(1)}, f32[2,1,2,256,128]{3,4,1,2,0:T(8,128)}, u32[]{:S(2)}) copy-start(f32[2,1,2,256,128]{3,4,1,2,0:T(8,128)} %copy.490) | copy-start | bytes 1572868
  319.3 24.9 %copy-start.3 = (f32[2,1,2,256,128]{3,4,1,2,0:T(8,128)S(1)}, f32[2,1,2,256,128]{3,4,1,2,0:T(8,128)}, u32[]{:S(2)}) copy-start(f32[2,1,2,256,128]{3,4,1,2,0:T(8,128)} %copy.492) | copy-start | bytes 1572868
  319.3 26.1 %copy-start.8 = (f32[1,256,2,256]{3,1,2,0:T(8,128)S(1)}, f32[1,256,2,256]{3,1,2,0:T(8,128)}, u32[]{:S(2)}) copy-start(f32[1,256,2,256]{3,1,2,0:T(8,128)} %get-tuple-element.46) | copy-start | bytes 1572868
  319.3 26.1 %copy-start.9 = (f32[1,256,2,256]{3,1,2,0:T(8,128)S(1)}, f32[1,256,2,256]{3,1,2,0:T(8,128)}, u32[]{:S(2)}) copy-start(f32[1,256,2,256]{3,1,2,0:T(8,128)} %get-tuple-element.55) | copy-start | bytes 1572868
  325.5 24.5 %copy-start.22 = (f32[2,2,32,128]{3,1,0,2:T(2,128)}, f32[2,2,32,128]{3,1,0,2:T(2,128)S(1)}, u32[]{:S(2)}) copy-start(f32[2,2,32,128]{3,1,0,2:T(2,128)S(1)} %fusion.74) | copy-start | bytes 196612
  340.6 24.1 %copy-start.24 = (s32[64,8]{0,1:T(8,128)S(1)}, s32[64,8]{0,1:T(8,128)}, u32[]{:S(2)}) copy-start(s32[64,8]{0,1:T(8,128)} %param.17) | copy-start | bytes 6148
  350.0 31.4 %all-to-all-start = ((bf16[2,2,2,256,128]{4,1,2,0,3:T(2,128)(2,1)}), bf16[2,2,2,256,128]{4,1,2,0,3:T(2,128)(2,1)S(1)}, u32[]{:S(2)}, u32[]{:S(2)}) async-start(bf16[2,2,2,256,128]{4,1,2,0,3:T(2,128)(2,1)} %copy.404), calls=%async_computation | async-start | bytes 1048576 | tf_op jit(solution)/shard_map/all_to_all | solution.py:99
  366.9 108.2 %copy-start.14 = (f32[1,64,2,64]{3,1,2,0:T(8,128)}, f32[1,64,2,64]{3,1,2,0:T(8,128)S(1)}, u32[]{:S(2)}) copy-start(f32[1,64,2,64]{3,1,2,0:T(8,128)S(1)} %get-tuple-element.57) | copy-start | bytes 98308
  521.0 49.0 %copy-start.10 = (f32[2,2,32,128]{3,1,0,2:T(2,128)}, f32[2,2,32,128]{3,1,0,2:T(2,128)S(1)}, u32[]{:S(2)}) copy-start(f32[2,2,32,128]{3,1,0,2:T(2,128)S(1)} %reduce_sum.150) | copy-start | bytes 196612
  643.4 39.7 %copy-start.23 = (f32[2,2,32,128]{3,1,0,2:T(2,128)S(1)}, f32[2,2,32,128]{3,1,0,2:T(2,128)}, u32[]{:S(2)}) copy-start(f32[2,2,32,128]{3,1,0,2:T(2,128)} %copy-done.22) | copy-start | bytes 196612
  661.4 19.5 %all-to-all-start.11 = ((f32[256,1,1]{2,1,0:T(1,128)}), f32[256,1,1]{2,1,0:T(1,128)S(1)}, u32[]{:S(2)}, u32[]{:S(2)}) async-start(f32[256,1,1]{2,1,0:T(1,128)} %broadcast_in_dim.17), calls=%async_computation.11 | async-start | bytes 262144 | tf_op jit(solution)/shard_map/all_to_all | solution.py:130
  (20 other events, 290.6 us)
where the time goes:
time: 697 us; the launch traced here: 685 us
  blocking collectives  233 us (33%)
  matrix products  181 us (26%)
  local copies, waits for them, and re-layouts  123 us (18%)
  starting transfers between devices  57.9 us (8%)
  other arithmetic  46.4 us (7%)
  waiting for transfers between devices  36.7 us (5%)
    conv_general_dilated x3, matrix products, conv_layer(): lax.conv_general_dilated(padded[None], kernel, (1, 1, 1), ((0, 0), (0, 0)...  156 us
    all_to_all x3, blocking collectives, coil_term(): lax.all_to_all(back.astype(jnp.bfloat16), 'slab', split_axis=2, concat_ax...  60.9 us
    all_to_all x3, blocking collectives, combine_coils(): lax.all_to_all(partial_value, 'coil', split_axis=2, concat_axis=0, tiled=...  48.8 us
    all_to_all x2, blocking collectives, coil_term(): lax.all_to_all(spectrum.astype(jnp.bfloat16), 'slab', split_axis=3, conca...  42.1 us
    all_gather x3, blocking collectives, gather_rows(): return lax.all_gather(value, 'coil', axis=2, tiled=True)  42 us
    all_to_all x2, blocking collectives, global_sums(): lax.all_to_all(spread, axes, split_axis=0, concat_axis=0, tiled=True)  39 us
    ppermute x6, starting transfers between devices, extended(): lax.ppermute(tail, axis, [(i, (i + 1) % count) for i in range(ends)])  27 us
    conv_general_dilated x9, local copies, waits for them, and re-layouts, conv_layer(): lax.conv_general_dilated(padded[None], kernel, (1, 1, 1), ((0, 0), (0, 0)...  26 us
  transfers between devices with their start and end apart: 14, of which 8 were waited for; matrix products, arithmetic and copies ran while one was open for 4% of the time, Pallas kernels for 0%

commit v1 on v0

--- a/solution.py
+++ b/solution.py
@@ -9,6 +9,30 @@
 STRIDE = 20
 REG_WEIGHT = 0.5
 HIGHEST_PRECISION = lax.Precision.HIGHEST
+
+
+def state_change(work_x):
+    y = lax.axis_size("coil")
+    finding = lax.axis_index("coil")
+    u1, y_new, k_now = (y, finding, work_x.shape[2])
+    vec_out = jnp.zeros(
+        [kk * u1 if dev == 2 else kk for dev, kk in enumerate(work_x.shape)], work_x.dtype
+    )
+    far_arr = lax.dynamic_update_slice_in_dim(vec_out, work_x, y_new * k_now, axis=2)
+    found_now = local_out = work_x
+    for t in range(1, u1 // 2 + 1):
+        found_now = lax.ppermute(found_now, "coil", [(dev, (dev + 1) % u1) for dev in range(u1)])
+        far_arr = lax.dynamic_update_slice_in_dim(
+            far_arr, found_now, (y_new - t) % u1 * k_now, axis=2
+        )
+        if 2 * t < u1:
+            local_out = lax.ppermute(
+                local_out, "coil", [(dev, (dev - 1) % u1) for dev in range(u1)]
+            )
+            far_arr = lax.dynamic_update_slice_in_dim(
+                far_arr, local_out, (y_new + t) % u1 * k_now, axis=2
+            )
+    return far_arr
 
 
 def extended(cells, sides, width):
@@ -120,7 +144,7 @@
 
 
 def gather_rows(value):
-    return lax.all_gather(value, "coil", axis=2, tiled=True)
+    return state_change(value)
 
 
 def global_sums(values):

time: 697 us -> 788 us (1.13)
  local copies, waits for them, and re-layouts: 123 us -> 203 us
  blocking collectives: 233 us -> 194 us
  starting transfers between devices: 57.9 us -> 92.8 us
  waiting for transfers between devices: 36.7 us -> 56.2 us
    dynamic_update_slice x0 -> x24, local copies, waits for them, and re-layouts: none -> 55.4 us  [the longest x12 25.9 us: state_change(): lax.dynamic_update_slice_in_dim(far_arr, found_now, (y_new - t) % u1 * k_...]
    all_gather x3 -> x0, blocking collectives: 42 us -> none  [gather_rows(): return lax.all_gather(value, 'coil', axis=2, tiled=True)]
    ppermute x0 -> x21, local copies, waits for them, and re-layouts: none -> 34.8 us  [the longest x12 19.5 us: state_change(): lax.ppermute(found_now, 'coil', [(dev, (dev + 1) % u1) for dev in range(u...]
    ppermute x0 -> x21, starting transfers between devices: none -> 22.5 us  [the longest x12 16.8 us: state_change(): lax.ppermute(found_now, 'coil', [(dev, (dev + 1) % u1) for dev in range(u...]
    all_to_all x3, blocking collectives: 48.8 us -> 62.1 us  [combine_coils(): lax.all_to_all(partial_value, 'coil', split_axis=2, concat_axis=0, tiled=...]
    ppermute x6, starting transfers between devices: 27 us -> 38 us  [extended(): lax.ppermute(tail, axis, [(i, (i + 1) % count) for i in range(ends)])]
    mul x9 -> x3, local copies, waits for them, and re-layouts: 13.6 us -> 3.19 us  [times_sens(): real_part = sens[:, 0] * image[0] - sens[:, 1] * image[1]]
    ppermute x6, waiting for transfers between devices: 11.5 us -> 20.1 us  [extended(): lax.ppermute(head, axis, [((i + 1) % count, i) for i in range(ends)])]
  transfers between devices with their start and end apart: 14 -> 35, of which waited for: 8 -> 22; matrix products, arithmetic and copies ran while one was open for 4% -> 14% of each run, Pallas kernels for 0% -> 0%
where the time goes in v1:
time: 788 us; the launch traced here: 775 us
  local copies, waits for them, and re-layouts  203 us (26%)
  blocking collectives  194 us (25%)
  matrix products  182 us (23%)
  starting transfers between devices  92.8 us (12%)
  waiting for transfers between devices  56.2 us (7%)
  other arithmetic  39.9 us (5%)
    conv_general_dilated x3, matrix products, conv_layer(): lax.conv_general_dilated(padded[None], kernel, (1, 1, 1), ((0, 0), (0, 0)...  155 us
    all_to_all x3, blocking collectives, combine_coils(): lax.all_to_all(partial_value, 'coil', split_axis=2, concat_axis=0, tiled=...  62.1 us
    all_to_all x3, blocking collectives, coil_term(): lax.all_to_all(back.astype(jnp.bfloat16), 'slab', split_axis=2, concat_ax...  57.8 us
    all_to_all x2, blocking collectives, global_sums(): lax.all_to_all(spread, axes, split_axis=0, concat_axis=0, tiled=True)  39.8 us
    ppermute x6, starting transfers between devices, extended(): lax.ppermute(tail, axis, [(i, (i + 1) % count) for i in range(ends)])  38 us
    all_to_all x2, blocking collectives, coil_term(): lax.all_to_all(spectrum.astype(jnp.bfloat16), 'slab', split_axis=3, conca...  34.8 us
    dynamic_update_slice x12, local copies, waits for them, and re-layouts, state_change(): lax.dynamic_update_slice_in_dim(far_arr, found_now, (y_new - t) % u1 * k_...  25.9 us
    conv_general_dilated x9, local copies, waits for them, and re-layouts, conv_layer(): lax.conv_general_dilated(padded[None], kernel, (1, 1, 1), ((0, 0), (0, 0)...  24.3 us
  transfers between devices with their start and end apart: 35, of which 22 were waited for; matrix products, arithmetic and copies ran while one was open for 14% of the time, Pallas kernels for 0%

profile of v1, /device:TPU:1, one launch (start us, length us, event | category | flops | bytes accessed | tf_op | source)
XLA Modules:
  0.0 774.8 jit_solution(18273814597511565372)
XLA Ops:
  10.0 5.2 collective-permute-start.2
  22.7 7.8 %broadcast_select_fusion.1 = f32[2,32,8,17,32]{4,2,3,1,0:T(8,128)S(1)} fusion(pred[8,17]{0,1:T(8,128)(4,1)} %constant.200, bf16[3,3,3,32,2]{3,4,2,1,0:T(2,128)(2,1)} %param.11, bf16[2,4,34,1,7,2]{4,0,5,2,1,3:T(2,128)(2,1)S(1)} %slice.155, bf16[2,4,34,1,8,17]{4,0,5,2,1,3:T(2,128)(2,1)S(1)} %copy.504), kind=kOutput, calls=%fused_computation.23 | convolution fusion | flops 30607616 | bytes 1199304 | tf_op jit(solution)/shard_map/conv_general_dilated | solution.py:71
  36.8 14.9 %collective-permute-start.4 = (bf16[32,1,32,128]{3,2,1,0:T(8,128)(2,1)S(1)}, bf16[32,1,32,128]{3,2,1,0:T(8,128)(2,1)}, u32[]{:S(2)}, u32[]{:S(2)}) collective-permute-start(bf16[32,1,32,128]{3,2,1,0:T(8,128)(2,1)S(1)} %copy.506), channel_id=1, source_target_pairs={{0,8},{8,16},{16,24},{24,32},{32,40},{40,48},{48,56},{56,64},{64,7... | collective-permute-start | bytes 786440 | tf_op jit(solution)/shard_map/ppermute | solution.py:46
  86.2 8.1 %copy.641 = bf16[32,4,34,1,128]{2,0,4,1,3:T(8,128)(2,1)} copy(bf16[32,4,34,1,128]{0,2,4,1,3:T(8,128)(2,1)} %maximum_bitcast_fusion) | data formatting | bytes 2228224
  99.5 8.8 %copy.512 = bf16[32,4,34,1,8,17]{0,4,5,2,1,3:T(8,128)(2,1)} copy(bf16[32,4,34,1,8,17]{2,0,5,4,1,3:T(8,128)(2,1)} %bitcast.328) | data formatting | bytes 2367488 | tf_op jit(solution)/shard_map/conv_general_dilated | solution.py:71
  109.5 8.6 %broadcast_select_fusion = f32[2,32,8,17,32]{4,2,3,1,0:T(8,128)S(1)} fusion(pred[8,17]{0,1:T(8,128)(4,1)S(1)} %copy-done.25, bf16[3,3,3,32,32]{4,3,2,1,0:T(8,128)(2,1)S(1)} %copy-done.26, bf16[32,4,34,1,7,2]{0,4,5,2,1,3:T(8,128)(2,1)S(1)} %slice.159, bf16[32,4,34,1,8,17]{0,4,5,2,1,3:T(8,128)(2,1)} %copy.512), kind=kOutput, calls=%fused_computation.22 | convolution fusion | flops 485543936 | bytes 2475144 | tf_op jit(solution)/shard_map/conv_general_dilated | solution.py:71
  160.7 6.3 maximum_bitcast_fusion.1
  167.0 8.1 %copy.642 = bf16[32,4,34,1,128]{2,0,4,1,3:T(8,128)(2,1)} copy(bf16[32,4,34,1,128]{0,2,4,1,3:T(8,128)(2,1)} %maximum_bitcast_fusion.1) | data formatting | bytes 2228224
  180.3 8.7 %copy.520 = bf16[32,4,34,1,8,17]{0,4,5,2,1,3:T(8,128)(2,1)} copy(bf16[32,4,34,1,8,17]{2,0,5,4,1,3:T(8,128)(2,1)} %bitcast.327) | data formatting | bytes 2367488 | tf_op jit(solution)/shard_map/conv_general_dilated | solution.py:71
  190.2 139.0 %fusion.11 = f32[2,32,8,17,2]{2,4,3,1,0:T(2,128)S(1)} fusion(bf16[3,3,3,2,32]{4,3,2,1,0:T(2,128)(2,1)S(1)} %copy-done.27, bf16[32,4,34,1,7,2]{0,4,5,2,1,3:T(8,128)(2,1)S(1)} %slice.163, bf16[32,4,34,1,8,17]{0,4,5,2,1,3:T(8,128)(2,1)} %copy.520), kind=kOutput, calls=%fused_computation.11 | convolution fusion | flops 34050048 | bytes 1378688 | tf_op jit(solution)/shard_map/conv_general_dilated | solution.py:71
  382.8 15.3 %all-to-all-start = ((bf16[2,2,2,256,128]{4,1,2,0,3:T(2,128)(2,1)}), bf16[2,2,2,256,128]{4,1,2,0,3:T(2,128)(2,1)}, u32[]{:S(2)}, u32[]{:S(2)}) async-start(bf16[2,2,2,256,128]{4,1,2,0,3:T(2,128)(2,1)} %copy.536), calls=%async_computation | async-start | bytes 1048576 | tf_op jit(solution)/shard_map/all_to_all | solution.py:123
  402.3 12.5 %all-to-all-done = bf16[2,2,2,256,128]{4,1,2,0,3:T(2,128)(2,1)} async-done(((bf16[2,2,2,256,128]{4,1,2,0,3:T(2,128)(2,1)}), bf16[2,2,2,256,128]{4,1,2,0,3:T(2,128)(2,1)}, u32[]{:S(2)}, u32[]{:S(2)}) %all-to-all-start) | async-done | bytes 524320 | tf_op jit(solution)/shard_map/all_to_all | solution.py:123
  419.6 20.3 %all_to_all.162 = bf16[2,2,64,8,128]{4,1,3,0,2:T(2,128)(2,1)S(1)} all-to-all(bf16[2,2,64,8,128]{4,1,3,0,2:T(2,128)(2,1)S(1)} %copy.540), channel_id=1, replica_groups=mesh['slab'=32,'coil'=8] {'slab'}, dimensions={2} | all-to-all | bytes 1048576 | tf_op jit(solution)/shard_map/all_to_all | solution.py:132
  444.3 16.8 %all_to_all.167 = f32[2,2,256,128]{3,1,0,2:T(2,128)} all-to-all(f32[2,2,256,128]{3,1,0,2:T(2,128)} %copy.544), channel_id=1, replica_groups=mesh['slab'=32,'coil'=8] {'coil'}, dimensions={2} | all-to-all | bytes 1048576 | tf_op jit(solution)/shard_map/all_to_all | solution.py:141
  513.9 17.5 %all_to_all.163 = bf16[2,2,2,256,128]{4,1,2,0,3:T(2,128)(2,1)S(1)} all-to-all(bf16[2,2,2,256,128]{4,1,2,0,3:T(2,128)(2,1)} %copy.553), channel_id=1, replica_groups=mesh['slab'=32,'coil'=8] {'slab'}, dimensions={3} | all-to-all | bytes 1048576 | tf_op jit(solution)/shard_map/all_to_all | solution.py:123
  534.8 18.7 %all_to_all.164 = bf16[2,2,64,8,128]{4,1,3,0,2:T(2,128)(2,1)S(1)} all-to-all(bf16[2,2,64,8,128]{4,1,3,0,2:T(2,128)(2,1)S(1)} %copy.557), channel_id=1, replica_groups=mesh['slab'=32,'coil'=8] {'slab'}, dimensions={2} | all-to-all | bytes 1048576 | tf_op jit(solution)/shard_map/all_to_all | solution.py:132
  558.0 22.7 %all_to_all.168 = f32[2,2,256,128]{3,1,0,2:T(2,128)} all-to-all(f32[2,2,256,128]{3,1,0,2:T(2,128)} %copy.561), channel_id=1, replica_groups=mesh['slab'=32,'coil'=8] {'coil'}, dimensions={2} | all-to-all | bytes 1048576 | tf_op jit(solution)/shard_map/all_to_all | solution.py:141
  584.0 20.2 %all_to_all.169 = f32[256,1,2]{2,1,0:T(1,128)} all-to-all(f32[256,1,2]{2,1,0:T(1,128)S(1)} %broadcast_in_dim.15), channel_id=1, replica_groups=mesh['slab'=32,'coil'=8] {'slab','coil'}, dimensions={0} | all-to-all | bytes 4096 | tf_op jit(solution)/shard_map/all_to_all | solution.py:154
  609.5 19.6 %all_to_all.170 = f32[256,1,1]{2,1,0:T(1,128)} all-to-all(f32[256,1,1]{2,1,0:T(1,128)S(1)} %broadcast_in_dim.16), channel_id=1, replica_groups=mesh['slab'=32,'coil'=8] {'slab','coil'}, dimensions={0} | all-to-all | bytes 2048 | tf_op jit(solution)/shard_map/all_to_all | solution.py:154
  684.4 17.2 %all_to_all.165 = bf16[2,2,2,256,128]{4,1,2,0,3:T(2,128)(2,1)S(1)} all-to-all(bf16[2,2,2,256,128]{4,1,2,0,3:T(2,128)(2,1)} %copy.572), channel_id=1, replica_groups=mesh['slab'=32,'coil'=8] {'slab'}, dimensions={3} | all-to-all | bytes 1048576 | tf_op jit(solution)/shard_map/all_to_all | solution.py:123
  705.0 18.7 %all_to_all.166 = bf16[2,2,64,8,128]{4,1,3,0,2:T(2,128)(2,1)S(1)} all-to-all(bf16[2,2,64,8,128]{4,1,3,0,2:T(2,128)(2,1)S(1)} %copy.576), channel_id=1, replica_groups=mesh['slab'=32,'coil'=8] {'slab'}, dimensions={2} | all-to-all | bytes 1048576 | tf_op jit(solution)/shard_map/all_to_all | solution.py:132
  725.6 22.6 %all_to_all.171 = f32[2,2,256,128]{3,1,0,2:T(2,128)S(1)} all-to-all(f32[2,2,256,128]{3,1,0,2:T(2,128)S(1)} %copy.580), channel_id=1, replica_groups=mesh['slab'=32,'coil'=8] {'coil'}, dimensions={2} | all-to-all | bytes 1048576 | tf_op jit(solution)/shard_map/all_to_all | solution.py:141
  750.4 7.4 all-to-all-start.11
  758.1 12.6 %all-to-all-done.11 = f32[256,1,1]{2,1,0:T(1,128)S(1)} async-done(((f32[256,1,1]{2,1,0:T(1,128)}), f32[256,1,1]{2,1,0:T(1,128)S(1)}, u32[]{:S(2)}, u32[]{:S(2)}) %all-to-all-start.11) | async-done | bytes 1056 | tf_op jit(solution)/shard_map/all_to_all | solution.py:154
  (290 shorter events, 310.5 us)
Async XLA Ops:
  1.6 5.9 collective-permute-start
  5.5 4.5 collective-permute-start.1
  10.0 8.1 %collective-permute-start.2 = (bf16[2,4,1,128]{3,2,1,0:T(2,128)(2,1)S(1)}, bf16[2,4,1,128]{3,2,1,0:T(2,128)(2,1)S(1)}, u32[]{:S(2)}, u32[]{:S(2)}) collective-permute-start(bf16[2,4,1,128]{3,2,1,0:T(2,128)(2,1)S(1)} %get-tuple-element.62), channel_id=1, source_target_pairs={{0,1},{1,2},{2,3},{3,4},{4,5},{5,6},{6,7},{8,9},{9,10},{10,11},{11... | collective-permute-start | bytes 6152 | tf_op jit(solution)/shard_map/ppermute | solution.py:46
  15.2 4.9 collective-permute-start.3
  36.8 19.5 %collective-permute-start.4 = (bf16[32,1,32,128]{3,2,1,0:T(8,128)(2,1)S(1)}, bf16[32,1,32,128]{3,2,1,0:T(8,128)(2,1)}, u32[]{:S(2)}, u32[]{:S(2)}) collective-permute-start(bf16[32,1,32,128]{3,2,1,0:T(8,128)(2,1)S(1)} %copy.506), channel_id=1, source_target_pairs={{0,8},{8,16},{16,24},{24,32},{32,40},{40,48},{48,56},{56,64},{64,7... | collective-permute-start | bytes 786440 | tf_op jit(solution)/shard_map/ppermute | solution.py:46
  55.1 9.1 %collective-permute-start.5 = (bf16[32,1,32,128]{3,2,1,0:T(8,128)(2,1)}, bf16[32,1,32,128]{3,2,1,0:T(8,128)(2,1)}, u32[]{:S(2)}, u32[]{:S(2)}) collective-permute-start(bf16[32,1,32,128]{3,2,1,0:T(8,128)(2,1)} %copy.507), channel_id=1, source_target_pairs={{8,0},{16,8},{24,16},{32,24},{40,32},{48,40},{56,48},{64,56},{72,6... | collective-permute-start | bytes 786440 | tf_op jit(solution)/shard_map/ppermute | solution.py:48
  69.7 7.4 collective-permute-start.6
  73.8 7.7 collective-permute-start.7
  125.9 9.4 %collective-permute-start.8 = (bf16[32,1,32,128]{3,2,1,0:T(8,128)(2,1)S(1)}, bf16[32,1,32,128]{3,2,1,0:T(8,128)(2,1)}, u32[]{:S(2)}, u32[]{:S(2)}) collective-permute-start(bf16[32,1,32,128]{3,2,1,0:T(8,128)(2,1)S(1)} %copy.514), channel_id=1, source_target_pairs={{0,8},{8,16},{16,24},{24,32},{32,40},{40,48},{48,56},{56,64},{64,7... | collective-permute-start | bytes 786440 | tf_op jit(solution)/shard_map/ppermute | solution.py:46
  134.0 7.4 collective-permute-start.9
  147.6 8.7 %collective-permute-start.10 = (bf16[32,4,1,128]{0,2,3,1:T(2,128)(2,1)}, bf16[32,4,1,128]{0,2,3,1:T(2,128)(2,1)S(1)}, u32[]{:S(2)}, u32[]{:S(2)}) collective-permute-start(bf16[32,4,1,128]{0,2,3,1:T(2,128)(2,1)} %get-tuple-element.26), channel_id=1, source_target_pairs={{0,1},{1,2},{2,3},{3,4},{4,5},{5,6},{6,7},{8,9},{9,10},{10,11},{11... | collective-permute-start | bytes 98312 | tf_op jit(solution)/shard_map/ppermute | solution.py:46
  152.7 8.0 %collective-permute-start.11 = (bf16[32,4,1,128]{0,2,3,1:T(2,128)(2,1)}, bf16[32,4,1,128]{0,2,3,1:T(2,128)(2,1)}, u32[]{:S(2)}, u32[]{:S(2)}) collective-permute-start(bf16[32,4,1,128]{0,2,3,1:T(2,128)(2,1)} %get-tuple-element.27), channel_id=1, source_target_pairs={{1,0},{2,1},{3,2},{4,3},{5,4},{6,5},{7,6},{9,8},{10,9},{11,10},{12... | collective-permute-start | bytes 98312 | tf_op jit(solution)/shard_map/ppermute | solution.py:48
  340.0 28.3 %collective-permute-start.17 = (f32[2,2,32,128]{3,1,0,2:T(2,128)}, f32[2,2,32,128]{3,1,0,2:T(2,128)}, u32[]{:S(2)}, u32[]{:S(2)}) collective-permute-start(f32[2,2,32,128]{3,1,0,2:T(2,128)} %collective-permute-done.15), channel_id=1, source_target_pairs={{0,7},{1,0},{2,1},{3,2},{4,3},{5,4},{6,5},{7,6},{8,15},{9,8},{10,9... | collective-permute-start | bytes 196616 | tf_op jit(solution)/shard_map/ppermute | solution.py:29
  340.0 31.8 %collective-permute-start.18 = (f32[2,2,32,128]{3,1,0,2:T(2,128)}, f32[2,2,32,128]{3,1,0,2:T(2,128)}, u32[]{:S(2)}, u32[]{:S(2)}) collective-permute-start(f32[2,2,32,128]{3,1,0,2:T(2,128)} %collective-permute-done.16), channel_id=1, source_target_pairs={{0,1},{1,2},{2,3},{3,4},{4,5},{5,6},{6,7},{7,0},{8,9},{9,10},{10,1... | collective-permute-start | bytes 196616 | tf_op jit(solution)/shard_map/ppermute | solution.py:24
  382.8 32.0 %all-to-all-start = ((bf16[2,2,2,256,128]{4,1,2,0,3:T(2,128)(2,1)}), bf16[2,2,2,256,128]{4,1,2,0,3:T(2,128)(2,1)}, u32[]{:S(2)}, u32[]{:S(2)}) async-start(bf16[2,2,2,256,128]{4,1,2,0,3:T(2,128)(2,1)} %copy.536), calls=%async_computation | async-start | bytes 1048576 | tf_op jit(solution)/shard_map/all_to_all | solution.py:123
  464.9 4.1 collective-permute-start.21
  469.0 5.0 collective-permute-start.23
  472.2 27.2 %collective-permute-start.24 = (f32[2,2,32,128]{3,1,0,2:T(2,128)}, f32[2,2,32,128]{3,1,0,2:T(2,128)}, u32[]{:S(2)}, u32[]{:S(2)}) collective-permute-start(f32[2,2,32,128]{3,1,0,2:T(2,128)} %collective-permute-done.22), channel_id=1, source_target_pairs={{0,7},{1,0},{2,1},{3,2},{4,3},{5,4},{6,5},{7,6},{8,15},{9,8},{10,9... | collective-permute-start | bytes 196616 | tf_op jit(solution)/shard_map/ppermute | solution.py:29
  474.1 28.8 %collective-permute-start.25 = (f32[2,2,32,128]{3,1,0,2:T(2,128)}, f32[2,2,32,128]{3,1,0,2:T(2,128)}, u32[]{:S(2)}, u32[]{:S(2)}) collective-permute-start(f32[2,2,32,128]{3,1,0,2:T(2,128)} %collective-permute-done.23), channel_id=1, source_target_pairs={{0,1},{1,2},{2,3},{3,4},{4,5},{5,6},{6,7},{7,0},{8,9},{9,10},{10,1... | collective-permute-start | bytes 196616 | tf_op jit(solution)/shard_map/ppermute | solution.py:24
  635.3 4.2 collective-permute-start.28
  639.6 5.0 collective-permute-start.30
  642.4 27.4 %collective-permute-start.31 = (f32[2,2,32,128]{3,1,0,2:T(2,128)}, f32[2,2,32,128]{3,1,0,2:T(2,128)}, u32[]{:S(2)}, u32[]{:S(2)}) collective-permute-start(f32[2,2,32,128]{3,1,0,2:T(2,128)} %collective-permute-done.29), channel_id=1, source_target_pairs={{0,7},{1,0},{2,1},{3,2},{4,3},{5,4},{6,5},{7,6},{8,15},{9,8},{10,9... | collective-permute-start | bytes 196616 | tf_op jit(solution)/shard_map/ppermute | solution.py:29
  644.6 28.7 %collective-permute-start.32 = (f32[2,2,32,128]{3,1,0,2:T(2,128)}, f32[2,2,32,128]{3,1,0,2:T(2,128)}, u32[]{:S(2)}, u32[]{:S(2)}) collective-permute-start(f32[2,2,32,128]{3,1,0,2:T(2,128)} %collective-permute-done.30), channel_id=1, source_target_pairs={{0,1},{1,2},{2,3},{3,4},{4,5},{5,6},{6,7},{7,0},{8,9},{9,10},{10,1... | collective-permute-start | bytes 196616 | tf_op jit(solution)/shard_map/ppermute | solution.py:24
  750.4 20.4 %all-to-all-start.11 = ((f32[256,1,1]{2,1,0:T(1,128)}), f32[256,1,1]{2,1,0:T(1,128)S(1)}, u32[]{:S(2)}, u32[]{:S(2)}) async-start(f32[256,1,1]{2,1,0:T(1,128)} %broadcast_in_dim.17), calls=%async_computation.11 | async-start | bytes 262144 | tf_op jit(solution)/shard_map/all_to_all | solution.py:154
  (41 other events, 1073.7 us)
